TPU v7x, 512 devices: a whole 4x8x8 slice. The times are simulated.
512 devices in a mesh: blk: 64 (over x, z, y_hi), dp: 8 (over y_lo, core).
Axes of the slice: x: 4, y: 8 (y_hi: 2, y_lo: 4; y = y_hi * 4 + y_lo), z: 8, core: 2. Of those that a mesh axis runs over, the one named last changes fastest.
Arguments:
- input_field: bfloat16 [262144, 2048], P('blk', 'dp'), may hold values from -6 to 6
- target_field: bfloat16 [262144, 2048], P('blk', 'dp'), may hold values from -6 to 6
- first_factor: bfloat16 [256, 1024, 256], P('dp', 'blk'), may hold values from -0.375 to 0.375
- second_factor: bfloat16 [256, 1024, 256], P('dp', 'blk'), may hold values from -0.375 to 0.375
Outputs:
- first_grad: bfloat16 [256, 1024, 256], P('dp', 'blk')
- second_grad: bfloat16 [256, 1024, 256], P('dp', 'blk')
All inputs are finite; a program needn't handle non-finite values.
Results may differ from a plain program's by a relative error of at most 0.012.
Values may be sent and summed in bfloat16 or wider, within the bound.
No kernel may reach another device: no remote copies, remote signals or barrier semaphores. Data moves between devices by JAX's collectives and lax.ppermute only.
A program may use at most 64 MiB of HBM per device.

v0:
```python
import math
import jax
import jax.numpy as jnp
from jax import lax
from jax.experimental.layout import Layout, with_layout_constraint
from jax.sharding import Mesh
from jax.sharding import PartitionSpec as P

NB = 1024
BS = 256
tanh_scale = 0.7978845608028654
cubic_coef = 0.044715


def gelu_value(values):
    inner = jnp.tanh(tanh_scale * (values + cubic_coef * values * values * values))
    return 0.5 * values * (1.0 + inner)


def gelu_slope(values):
    inner = jnp.tanh(tanh_scale * (values + cubic_coef * values * values * values))
    return 0.5 * (1.0 + inner) + 0.5 * values * (1.0 - inner * inner) * tanh_scale * (
        1.0 + 3.0 * cubic_coef * values * values
    )


def line_pairs(n, step):
    return [(i, i + step) for i in range(n) if 0 <= i + step < n]


def swap_pairs(n):
    return [(c, (c + 1) % n) for c in range(n)]


def swap_pairs(n):
    return [(c, (c + 1) % n) for c in range(n)]


def gather_rows(piece):
    n_core = lax.axis_size("core")
    n_ylo = lax.axis_size("ylo")
    c = lax.axis_index("core")
    copies = jnp.broadcast_to(piece[None], (n_ylo,) + piece.shape)
    line = lax.all_to_all(copies, "ylo", split_axis=0, concat_axis=0, tiled=True)
    other = lax.ppermute(line, "core", swap_pairs(n_core))
    pair = jnp.zeros((n_ylo, n_core) + piece.shape, piece.dtype)
    pair = lax.dynamic_update_index_in_dim(pair, line, c, 1)
    pair = lax.dynamic_update_index_in_dim(pair, other, lax.rem(c + 1, n_core), 1)
    return pair.reshape((n_ylo * n_core * piece.shape[0],) + piece.shape[1:])


def scatter_rows(term):
    n_core = lax.axis_size("core")
    n_ylo = lax.axis_size("ylo")
    c = lax.axis_index("core")
    blocks, total_rows, width = term.shape
    rows = total_rows // (n_core * n_ylo)
    split = term.reshape(blocks, n_ylo, n_core, rows, width)
    sent = lax.dynamic_index_in_dim(split, lax.rem(c + 1, n_core), 2, keepdims=False)
    kept = lax.dynamic_index_in_dim(split, c, 2, keepdims=False)
    got = lax.ppermute(sent, "core", swap_pairs(n_core))
    half = (kept.astype(jnp.float32) + got.astype(jnp.float32)).astype(jnp.bfloat16)
    arrived = lax.all_to_all(half, "ylo", split_axis=1, concat_axis=1, tiled=True)
    total = jnp.sum(arrived.astype(jnp.float32), axis=1).astype(jnp.bfloat16)
    return jnp.transpose(total, (1, 0, 2))


def shards(input_field, target_field, first_factor, second_factor):
    block_count = first_factor.shape[1]
    block_size = first_factor.shape[2]
    row_count = input_field.shape[1]
    dp = ("ylo", "core")
    replica_count = lax.axis_size("ylo") * lax.axis_size("core")
    blk_count = lax.axis_size("blk")
    group_count = NB // BS
    inner_count = block_count // group_count
    scale_factor = 1.0 / math.sqrt(row_count * replica_count)
    inputs = input_field.reshape(block_count, block_size, row_count)
    first_full = gather_rows(first_factor)
    second_full = lax.all_gather(second_factor, dp, axis=0, tiled=True)
    pre_act = jnp.einsum("bkr,kbi->bir", inputs, first_full, preferred_element_type=jnp.float32)
    pre_split = pre_act.reshape(block_count, blk_count, inner_count, row_count)
    activated = gelu_value(pre_split).astype(jnp.bfloat16)
    slope = jnp.transpose(gelu_slope(pre_split).astype(jnp.bfloat16), (2, 1, 0, 3))
    activated, second_full, slope = lax.optimization_barrier((activated, second_full, slope))
    sending = jnp.transpose(activated, (2, 1, 0, 3))
    sending = with_layout_constraint(sending, Layout((1, 0, 2, 3)))
    received = lax.all_to_all(sending, "blk", split_axis=1, concat_axis=1, tiled=True)
    permuted = received.reshape(block_count, block_size, row_count)
    targets = target_field.reshape(block_count, block_size, row_count)
    second_t = jnp.transpose(second_full, (1, 0, 2))
    predicted = jnp.einsum("qcj,qcr->qjr", second_t, permuted, preferred_element_type=jnp.float32)
    residual = ((predicted - targets.astype(jnp.float32)) * scale_factor).astype(jnp.bfloat16)
    permuted_grad = jnp.einsum(
        "qcj,qjr->qcr", second_t, residual, preferred_element_type=jnp.float32
    ).astype(jnp.bfloat16)
    term = jnp.einsum("qcr,qjr->cqj", permuted, residual, preferred_element_type=jnp.float32)
    second_out = lax.psum_scatter(term.astype(jnp.bfloat16), dp, scatter_dimension=0, tiled=True)
    back = permuted_grad.reshape(inner_count, blk_count, block_count, row_count)
    back = with_layout_constraint(back, Layout((1, 0, 2, 3)))
    activated_grad = lax.all_to_all(back, "blk", split_axis=1, concat_axis=1, tiled=True)
    pre_grad = (activated_grad.astype(jnp.float32) * slope).astype(jnp.bfloat16)
    pre_grad = jnp.transpose(pre_grad, (2, 1, 0, 3)).reshape(block_count, block_size, row_count)
    first_sum = scatter_rows(
        jnp.einsum("bkr,bir->bki", inputs, pre_grad, preferred_element_type=jnp.float32).astype(
            jnp.bfloat16
        )
    )
    return (first_sum, second_out)


def solution(mesh):
    n_blk, n_dp = mesh.devices.shape
    n_core = 2
    split_mesh = Mesh(mesh.devices.reshape(n_blk, n_dp // n_core, n_core), ("blk", "ylo", "core"))
    dp = ("ylo", "core")
    return jax.shard_map(
        shards,
        mesh=split_mesh,
        in_specs=(P("blk", dp), P("blk", dp), P(dp, "blk", None), P(dp, "blk", None)),
        out_specs=(P(dp, "blk", None), P(dp, "blk", None)),
        check_vma=False,
    )
```

profile of v0, /device:TPU:1, one launch (start us, length us, event | category | flops | bytes accessed | tf_op | source)
XLA Modules:
  0.0 266.5 jit_solution(7686284974705807812)
XLA Ops:
  7.2 0.0 copy-start
  7.2 2.2 broadcast_in_dim.17
  9.3 5.4 %all-to-all-start = ((bf16[4,32,16,256]{3,2,1,0:T(8,128)(2,1)}), bf16[4,32,16,256]{3,2,1,0:T(8,128)(2,1)S(1)}, u32[]{:S(2)}, u32[]{:S(2)}) async-start(bf16[4,32,16,256]{3,2,1,0:T(8,128)(2,1)} %broadcast_in_dim.17), calls=%async_computation | async-start | bytes 2097152 | tf_op jit(solution)/shard_map/all_to_all | solution.py:44
  14.8 0.0 all-gather.2.cloned.1.call-start
  14.8 0.7 all-gather.2.cloned.1.call-update
  15.5 22.9 %all-to-all-done = bf16[4,32,16,256]{3,2,1,0:T(8,128)(2,1)S(1)} async-done(((bf16[4,32,16,256]{3,2,1,0:T(8,128)(2,1)}), bf16[4,32,16,256]{3,2,1,0:T(8,128)(2,1)S(1)}, u32[]{:S(2)}, u32[]{:S(2)}) %all-to-all-start) | async-done | bytes 1048608 | tf_op jit(solution)/shard_map/all_to_all | solution.py:44
  38.4 9.8 %collective-permute-start = (bf16[4,32,16,256]{3,2,1,0:T(8,128)(2,1)S(1)}, bf16[4,32,16,256]{3,2,1,0:T(8,128)(2,1)}, u32[]{:S(2)}, u32[]{:S(2)}) collective-permute-start(bf16[4,32,16,256]{3,2,1,0:T(8,128)(2,1)S(1)} %all-to-all-done), channel_id=1, source_target_pairs={{0,1},{1,0},{2,3},{3,2},{4,5},{5,4},{6,7},{7,6},{8,9},{9,8},{10,11... | collective-permute-start | bytes 3145736 | tf_op jit(solution)/shard_map/ppermute | solution.py:45
  48.2 0.2 broadcast_in_dim.16
  48.4 0.1 bitcast_dynamic-update-slice_fusion.1
  48.5 2.1 collective-permute-done
  50.6 1.3 bitcast_dynamic-update-slice_fusion
  51.9 0.0 copy-done
  51.9 1.5 fusion.11
  53.5 2.4 copy.26
  55.9 4.2 %fusion.13 = (bf16[4,64,16,256]{3,2,0,1:T(8,128)(2,1)}, bf16[16,64,4,256]{3,0,2,1:T(8,128)(2,1)}) fusion(f32[16,64,4,256]{3,0,2,1:T(8,128)S(1)} %bitcast.46), kind=kLoop, calls=%fused_computation.20 | loop fusion | flops 20971520 | bytes 8388608 | tf_op jit(solution)/shard_map/transpose | solution.py:84
  60.0 1.9 all-gather.2.cloned.1.call-done
  62.0 73.9 %all_to_all.20 = bf16[4,64,16,256]{3,2,0,1:T(8,128)(2,1)S(1)} all-to-all(bf16[4,64,16,256]{3,2,0,1:T(8,128)(2,1)} %bitcast.52), channel_id=1, replica_groups=mesh['blk'=64,'ylo'=4,'core'=2] {'blk'}, dimensions={1} | all-to-all | bytes 4194304 | tf_op jit(solution)/shard_map/all_to_all | solution.py:88
  135.9 0.0 copy-start.3
  135.9 0.0 copy-start.4
  135.9 0.2 copy.27
  136.1 0.0 copy-start.2
  136.1 2.2 copy-done.3
  138.3 0.6 copy-done.4
  138.9 1.7 fusion.7
  140.6 0.0 copy-done.2
  140.6 0.0 copy-start.1
  140.6 0.9 convolution_convert_fusion
  141.5 0.5 copy-done.1
  142.0 1.6 copy.30
  143.6 7.7 %all-to-all-start.2 = ((bf16[4,64,16,256]{3,2,0,1:T(8,128)(2,1)}), bf16[4,64,16,256]{3,2,0,1:T(8,128)(2,1)}, u32[]{:S(2)}, u32[]{:S(2)}) async-start(bf16[4,64,16,256]{3,2,0,1:T(8,128)(2,1)} %copy.30), calls=%async_computation.2 | async-start | bytes 4194304 | tf_op jit(solution)/shard_map/all_to_all | solution.py:101
  151.3 0.2 reduce-scatter.2.cloned.1.call-start
  151.5 4.3 %convert_bitcast_fusion = bf16[256,16,256]{0,2,1:T(8,128)(2,1)} fusion(bf16[16,256,256]{2,1,0:T(8,128)(2,1)} %copy-done.1, bf16[16,256,256]{2,1,0:T(8,128)(2,1)} %bitcast.45), kind=kOutput, calls=%fused_computation.19 | convolution fusion | flops 537919488 | bytes 6291456 | tf_op jit(solution)/shard_map/qcr,qjr->cqj/dot_general | solution.py:97
  155.8 4.6 %copy.35 = bf16[256,16,256]{2,1,0:T(8,128)(2,1)} copy(bf16[256,16,256]{0,2,1:T(8,128)(2,1)} %convert_bitcast_fusion) | data formatting | bytes 4194304 | tf_op jit(solution)/shard_map/convert_element_type | solution.py:98
  160.4 0.0 reduce-scatter.2.cloned.1.call-update
  160.4 51.0 %all-to-all-done.2 = bf16[4,64,16,256]{3,2,0,1:T(8,128)(2,1)} async-done(((bf16[4,64,16,256]{3,2,0,1:T(8,128)(2,1)}), bf16[4,64,16,256]{3,2,0,1:T(8,128)(2,1)}, u32[]{:S(2)}, u32[]{:S(2)}) %all-to-all-start.2) | async-done | bytes 2097184 | tf_op jit(solution)/shard_map/all_to_all | solution.py:101
  211.5 3.2 %multiply_convert_fusion = bf16[4,64,16,256]{3,2,0,1:T(8,128)(2,1)S(1)} fusion(bf16[4,64,16,256]{3,2,0,1:T(8,128)(2,1)} %get-tuple-element.7, bf16[4,64,16,256]{3,2,0,1:T(8,128)(2,1)} %all-to-all-done.2), kind=kLoop, calls=%fused_computation.11 | loop fusion | flops 4194304 | bytes 6291456 | tf_op jit(solution)/shard_map/convert_element_type | solution.py:102
  214.7 1.0 fusion.14
  215.7 0.2 constant_dynamic-slice_fusion.1
  215.9 0.1 copy.53
  215.9 8.3 %collective-permute-start.1 = (bf16[16,4,32,256]{3,2,0,1:T(8,128)(2,1)S(1)}, bf16[16,4,32,256]{3,2,0,1:T(8,128)(2,1)S(1)}, u32[]{:S(2)}, u32[]{:S(2)}) collective-permute-start(bf16[16,4,32,256]{3,2,0,1:T(8,128)(2,1)S(1)} %bitcast.56), channel_id=1, source_target_pairs={{0,1},{1,0},{2,3},{3,2},{4,5},{5,4},{6,7},{7,6},{8,9},{9,8},{10,11... | collective-permute-start | bytes 3145736 | tf_op jit(solution)/shard_map/ppermute | solution.py:61
  224.3 2.3 collective-permute-done.1
  226.5 0.4 fusion.8
  227.0 31.6 %all_to_all.21 = bf16[16,4,32,256]{3,2,0,1:T(8,128)(2,1)S(1)} all-to-all(bf16[16,4,32,256]{3,2,0,1:T(8,128)(2,1)S(1)} %fusion.8), channel_id=1, replica_groups=mesh['blk'=64,'ylo'=4,'core'=2] {'ylo'}, dimensions={1} | all-to-all | bytes 2097152 | tf_op jit(solution)/shard_map/all_to_all | solution.py:63
  258.6 0.2 reduce_sum.12
  258.8 0.9 copy.36
  259.6 0.0 reduce-scatter.2.cloned.1.call-done
Async XLA Ops:
  7.2 44.8 %copy-start = (bf16[4096,256]{1,0:T(8,128)(2,1)S(1)}, bf16[4096,256]{1,0:T(8,128)(2,1)}, u32[]{:S(2)}) copy-start(bf16[4096,256]{1,0:T(8,128)(2,1)} %param.4) | copy-start | bytes 6291460
  9.3 29.0 %all-to-all-start = ((bf16[4,32,16,256]{3,2,1,0:T(8,128)(2,1)}), bf16[4,32,16,256]{3,2,1,0:T(8,128)(2,1)S(1)}, u32[]{:S(2)}, u32[]{:S(2)}) async-start(bf16[4,32,16,256]{3,2,1,0:T(8,128)(2,1)} %broadcast_in_dim.17), calls=%async_computation | async-start | bytes 2097152 | tf_op jit(solution)/shard_map/all_to_all | solution.py:44
  14.8 47.2 %all-gather.2.cloned.1.call-start = ((), (), s32[]{:S(2)}) async-start(), calls=%async_computation.5 | async-start | bytes 2359296 | tf_op jit(solution)/shard_map/all_gather | solution.py:80
  38.4 12.2 %collective-permute-start = (bf16[4,32,16,256]{3,2,1,0:T(8,128)(2,1)S(1)}, bf16[4,32,16,256]{3,2,1,0:T(8,128)(2,1)}, u32[]{:S(2)}, u32[]{:S(2)}) collective-permute-start(bf16[4,32,16,256]{3,2,1,0:T(8,128)(2,1)S(1)} %all-to-all-done), channel_id=1, source_target_pairs={{0,1},{1,0},{2,3},{3,2},{4,5},{5,4},{6,7},{7,6},{8,9},{9,8},{10,11... | collective-permute-start | bytes 3145736 | tf_op jit(solution)/shard_map/ppermute | solution.py:45
  135.9 2.3 copy-start.3
  135.9 3.0 %copy-start.4 = (bf16[4096,256]{1,0:T(8,128)(2,1)S(1)}, bf16[4096,256]{1,0:T(8,128)(2,1)}, u32[]{:S(2)}) copy-start(bf16[4096,256]{1,0:T(8,128)(2,1)} %param.5) | copy-start | bytes 6291460
  136.1 4.5 %copy-start.2 = (bf16[4,64,16,256]{3,2,1,0:T(8,128)(2,1)}, bf16[4,64,16,256]{3,2,1,0:T(8,128)(2,1)S(1)}, u32[]{:S(2)}) copy-start(bf16[4,64,16,256]{3,2,1,0:T(8,128)(2,1)S(1)} %copy.27) | copy-start | bytes 6291460
  140.6 1.4 copy-start.1
  143.6 67.9 %all-to-all-start.2 = ((bf16[4,64,16,256]{3,2,0,1:T(8,128)(2,1)}), bf16[4,64,16,256]{3,2,0,1:T(8,128)(2,1)}, u32[]{:S(2)}, u32[]{:S(2)}) async-start(bf16[4,64,16,256]{3,2,0,1:T(8,128)(2,1)} %copy.30), calls=%async_computation.2 | async-start | bytes 4194304 | tf_op jit(solution)/shard_map/all_to_all | solution.py:101
  151.3 108.4 %reduce-scatter.2.cloned.1.call-start = ((), (), s32[]{:S(2)}) async-start(), calls=%async_computation.6 | async-start | bytes 2359296 | tf_op jit(solution)/shard_map/reduce_scatter | solution.py:98
  215.9 10.6 %collective-permute-start.1 = (bf16[16,4,32,256]{3,2,0,1:T(8,128)(2,1)S(1)}, bf16[16,4,32,256]{3,2,0,1:T(8,128)(2,1)S(1)}, u32[]{:S(2)}, u32[]{:S(2)}) collective-permute-start(bf16[16,4,32,256]{3,2,0,1:T(8,128)(2,1)S(1)} %bitcast.56), channel_id=1, source_target_pairs={{0,1},{1,0},{2,3},{3,2},{4,5},{5,4},{6,7},{7,6},{8,9},{9,8},{10,11... | collective-permute-start | bytes 3145736 | tf_op jit(solution)/shard_map/ppermute | solution.py:61
Sparse Core Ops, SparseCore 0:
  17.7 44.2 all-gather.1
  160.6 60.7 reduce-scatter.1
where the time goes:
time: 267 us; the launch traced here: 266 us
  blocking collectives  106 us (40%)
  waiting for transfers between devices  81 us (30%)
  starting transfers between devices  31.5 us (12%)
  local copies, waits for them, and re-layouts  16.9 us (6%)
  between operations  14.2 us (5%)
  matrix products  9.36 us (4%)
  other arithmetic  7.96 us (3%)
    all_to_all x1, blocking collectives, shards(): lax.all_to_all(sending, 'blk', split_axis=1, concat_axis=1, tiled=True)  73.9 us
    all_to_all x1, waiting for transfers between devices, shards(): lax.all_to_all(back, 'blk', split_axis=1, concat_axis=1, tiled=True)  51 us
    all_to_all x1, blocking collectives, scatter_rows(): lax.all_to_all(half, 'ylo', split_axis=1, concat_axis=1, tiled=True)  31.6 us
    all_to_all x1, waiting for transfers between devices, gather_rows(): lax.all_to_all(copies, 'ylo', split_axis=0, concat_axis=0, tiled=True)  22.9 us
    ppermute x1, starting transfers between devices, gather_rows(): other = lax.ppermute(line, 'core', swap_pairs(n_core))  9.84 us
    ppermute x1, starting transfers between devices, scatter_rows(): got = lax.ppermute(sent, 'core', swap_pairs(n_core))  8.32 us
    all_to_all x1, starting transfers between devices, shards(): lax.all_to_all(back, 'blk', split_axis=1, concat_axis=1, tiled=True)  7.73 us
    all_to_all x1, starting transfers between devices, gather_rows(): lax.all_to_all(copies, 'ylo', split_axis=0, concat_axis=0, tiled=True)  5.42 us
  transfers between devices with their start and end apart: 6, of which 5 were waited for; matrix products, arithmetic and copies ran while one was open for 9% of the time, Pallas kernels for 0%

commit v1 on v0

--- a/solution.py
+++ b/solution.py
@@ -60,7 +60,15 @@
     kept = lax.dynamic_index_in_dim(split, c, 2, keepdims=False)
     got = lax.ppermute(sent, "core", swap_pairs(n_core))
     half = (kept.astype(jnp.float32) + got.astype(jnp.float32)).astype(jnp.bfloat16)
-    arrived = lax.all_to_all(half, "ylo", split_axis=1, concat_axis=1, tiled=True)
+    arrived = jnp.concatenate(
+        lax.all_to_all(
+            jnp.stack(jnp.split(half, lax.axis_size("ylo"), axis=1)),
+            axis_name="ylo",
+            split_axis=0,
+            concat_axis=0,
+        ),
+        axis=1,
+    )
     total = jnp.sum(arrived.astype(jnp.float32), axis=1).astype(jnp.bfloat16)
     return jnp.transpose(total, (1, 0, 2))
 

time: 267 us -> 264 us (0.989)
  waiting for transfers between devices: 81 us -> 78.3 us
    all_to_all x1, waiting for transfers between devices: 51 us -> 48.4 us  [shards(): lax.all_to_all(back, 'blk', split_axis=1, concat_axis=1, tiled=True)]
where the time goes in v1:
time: 264 us
  blocking collectives  104 us (39%)
  waiting for transfers between devices  78.3 us (30%)
  starting transfers between devices  32.8 us (12%)
  local copies, waits for them, and re-layouts  17 us (6%)
  between operations  14.2 us (5%)
  matrix products  9.36 us (4%)
  other arithmetic  8.08 us (3%)
    all_to_all x1, blocking collectives, shards(): lax.all_to_all(sending, 'blk', split_axis=1, concat_axis=1, tiled=True)  73.6 us
    all_to_all x1, waiting for transfers between devices, shards(): lax.all_to_all(back, 'blk', split_axis=1, concat_axis=1, tiled=True)  48.4 us
    all_to_all x1, blocking collectives, scatter_rows(): lax.all_to_all(jnp.stack(jnp.split(half, lax.axis_size('ylo'), axis=1)),...  30.3 us
    all_to_all x1, waiting for transfers between devices, gather_rows(): lax.all_to_all(copies, 'ylo', split_axis=0, concat_axis=0, tiled=True)  22.9 us
    ppermute x1, starting transfers between devices, scatter_rows(): got = lax.ppermute(sent, 'core', swap_pairs(n_core))  9.85 us
    ppermute x1, starting transfers between devices, gather_rows(): other = lax.ppermute(line, 'core', swap_pairs(n_core))  9.84 us
    all_to_all x1, starting transfers between devices, shards(): lax.all_to_all(back, 'blk', split_axis=1, concat_axis=1, tiled=True)  7.42 us
    all_to_all x1, starting transfers between devices, gather_rows(): lax.all_to_all(copies, 'ylo', split_axis=0, concat_axis=0, tiled=True)  5.42 us
  transfers between devices with their start and end apart: 6, of which 5 were waited for; matrix products, arithmetic and copies ran while one was open for 9% of the time, Pallas kernels for 0%

profile of v1, /device:TPU:1, one launch (start us, length us, event | category | flops | bytes accessed | tf_op | source)
XLA Modules:
  0.0 263.6 jit_solution(7122618577009928712)
XLA Ops:
  7.2 0.0 copy-start
  7.2 2.2 broadcast_in_dim.17
  9.3 5.4 %all-to-all-start = ((bf16[4,32,16,256]{3,2,1,0:T(8,128)(2,1)}), bf16[4,32,16,256]{3,2,1,0:T(8,128)(2,1)S(1)}, u32[]{:S(2)}, u32[]{:S(2)}) async-start(bf16[4,32,16,256]{3,2,1,0:T(8,128)(2,1)} %broadcast_in_dim.17), calls=%async_computation | async-start | bytes 2097152 | tf_op jit(solution)/shard_map/all_to_all | solution.py:44
  14.8 0.0 all-gather.2.cloned.1.call-start
  14.8 0.7 all-gather.2.cloned.1.call-update
  15.5 22.9 %all-to-all-done = bf16[4,32,16,256]{3,2,1,0:T(8,128)(2,1)S(1)} async-done(((bf16[4,32,16,256]{3,2,1,0:T(8,128)(2,1)}), bf16[4,32,16,256]{3,2,1,0:T(8,128)(2,1)S(1)}, u32[]{:S(2)}, u32[]{:S(2)}) %all-to-all-start) | async-done | bytes 1048608 | tf_op jit(solution)/shard_map/all_to_all | solution.py:44
  38.4 9.8 %collective-permute-start = (bf16[4,32,16,256]{3,2,1,0:T(8,128)(2,1)S(1)}, bf16[4,32,16,256]{3,2,1,0:T(8,128)(2,1)}, u32[]{:S(2)}, u32[]{:S(2)}) collective-permute-start(bf16[4,32,16,256]{3,2,1,0:T(8,128)(2,1)S(1)} %all-to-all-done), channel_id=1, source_target_pairs={{0,1},{1,0},{2,3},{3,2},{4,5},{5,4},{6,7},{7,6},{8,9},{9,8},{10,11... | collective-permute-start | bytes 3145736 | tf_op jit(solution)/shard_map/ppermute | solution.py:45
  48.2 0.2 broadcast_in_dim.16
  48.4 0.1 bitcast_dynamic-update-slice_fusion.1
  48.5 2.1 collective-permute-done
  50.6 1.3 bitcast_dynamic-update-slice_fusion
  51.9 0.0 copy-done
  52.0 1.5 fusion.11
  53.5 2.4 copy.32
  55.9 4.1 %fusion.13 = (bf16[4,64,16,256]{3,2,0,1:T(8,128)(2,1)}, bf16[16,64,4,256]{3,0,2,1:T(8,128)(2,1)}) fusion(f32[16,64,4,256]{3,0,2,1:T(8,128)S(1)} %bitcast.54), kind=kLoop, calls=%fused_computation.20 | loop fusion | flops 20971520 | bytes 8388608 | tf_op jit(solution)/shard_map/transpose | solution.py:92
  60.1 1.9 all-gather.2.cloned.1.call-done
  62.0 73.6 %all_to_all.20 = bf16[4,64,16,256]{3,2,0,1:T(8,128)(2,1)S(1)} all-to-all(bf16[4,64,16,256]{3,2,0,1:T(8,128)(2,1)} %bitcast.60), channel_id=1, replica_groups=mesh['blk'=64,'ylo'=4,'core'=2] {'blk'}, dimensions={1} | all-to-all | bytes 4194304 | tf_op jit(solution)/shard_map/all_to_all | solution.py:96
  135.6 0.0 copy-start.3
  135.6 0.0 copy-start.4
  135.6 0.2 copy.33
  135.7 0.0 copy-start.2
  135.7 2.2 copy-done.3
  137.9 0.6 copy-done.4
  138.5 1.7 fusion.7
  140.2 0.0 copy-done.2
  140.3 0.0 copy-start.1
  140.3 0.9 convolution_convert_fusion
  141.1 0.5 copy-done.1
  141.6 1.6 copy.36
  143.2 7.4 %all-to-all-start.2 = ((bf16[4,64,16,256]{3,2,0,1:T(8,128)(2,1)}), bf16[4,64,16,256]{3,2,0,1:T(8,128)(2,1)}, u32[]{:S(2)}, u32[]{:S(2)}) async-start(bf16[4,64,16,256]{3,2,0,1:T(8,128)(2,1)} %copy.36), calls=%async_computation.2 | async-start | bytes 4194304 | tf_op jit(solution)/shard_map/all_to_all | solution.py:109
  150.7 0.2 reduce-scatter.2.cloned.1.call-start
  150.9 4.3 %convert_bitcast_fusion = bf16[256,16,256]{0,2,1:T(8,128)(2,1)} fusion(bf16[16,256,256]{2,1,0:T(8,128)(2,1)} %copy-done.1, bf16[16,256,256]{2,1,0:T(8,128)(2,1)} %bitcast.53), kind=kOutput, calls=%fused_computation.19 | convolution fusion | flops 537919488 | bytes 6291456 | tf_op jit(solution)/shard_map/qcr,qjr->cqj/dot_general | solution.py:105
  155.2 4.6 %copy.40 = bf16[256,16,256]{2,1,0:T(8,128)(2,1)} copy(bf16[256,16,256]{0,2,1:T(8,128)(2,1)} %convert_bitcast_fusion) | data formatting | bytes 4194304 | tf_op jit(solution)/shard_map/convert_element_type | solution.py:106
  159.8 0.0 reduce-scatter.2.cloned.1.call-update
  159.8 48.4 %all-to-all-done.2 = bf16[4,64,16,256]{3,2,0,1:T(8,128)(2,1)} async-done(((bf16[4,64,16,256]{3,2,0,1:T(8,128)(2,1)}), bf16[4,64,16,256]{3,2,0,1:T(8,128)(2,1)}, u32[]{:S(2)}, u32[]{:S(2)}) %all-to-all-start.2) | async-done | bytes 2097184 | tf_op jit(solution)/shard_map/all_to_all | solution.py:109
  208.1 3.2 %multiply_convert_fusion = bf16[4,64,16,256]{3,2,0,1:T(8,128)(2,1)S(1)} fusion(bf16[4,64,16,256]{3,2,0,1:T(8,128)(2,1)} %get-tuple-element.7, bf16[4,64,16,256]{3,2,0,1:T(8,128)(2,1)} %all-to-all-done.2), kind=kLoop, calls=%fused_computation.11 | loop fusion | flops 4194304 | bytes 6291456 | tf_op jit(solution)/shard_map/convert_element_type | solution.py:110
  211.3 1.0 fusion.14
  212.3 0.2 constant_dynamic-slice_fusion.1
  212.5 0.1 copy.57
  212.6 9.8 %collective-permute-start.1 = (bf16[16,4,32,256]{3,2,0,1:T(8,128)(2,1)S(1)}, bf16[16,4,32,256]{3,2,0,1:T(8,128)(2,1)S(1)}, u32[]{:S(2)}, u32[]{:S(2)}) collective-permute-start(bf16[16,4,32,256]{3,2,0,1:T(8,128)(2,1)S(1)} %bitcast.64), channel_id=1, source_target_pairs={{0,1},{1,0},{2,3},{3,2},{4,5},{5,4},{6,7},{7,6},{8,9},{9,8},{10,11... | collective-permute-start | bytes 3145736 | tf_op jit(solution)/shard_map/ppermute | solution.py:61
  222.4 2.3 collective-permute-done.1
  224.7 0.4 fusion.8
  225.2 0.1 slice_bitcast_fusion.3
  225.2 0.1 pad_maximum_fusion
  225.4 30.3 %all_to_all.21 = bf16[4,16,1,32,256]{4,3,1,2,0:T(8,128)(2,1)S(1)} all-to-all(bf16[4,16,1,32,256]{4,3,1,2,0:T(8,128)(2,1)S(1)} %pad_maximum_fusion), channel_id=1, replica_groups=mesh['blk'=64,'ylo'=4,'core'=2] {'ylo'}, dimensions={0} | all-to-all | bytes 2097152 | tf_op jit(solution)/shard_map/all_to_all | solution.py:64
  255.7 0.2 reduce_sum.12
  255.9 0.9 copy.41
  256.8 0.0 reduce-scatter.2.cloned.1.call-done
Async XLA Ops:
  7.2 44.8 %copy-start = (bf16[4096,256]{1,0:T(8,128)(2,1)S(1)}, bf16[4096,256]{1,0:T(8,128)(2,1)}, u32[]{:S(2)}) copy-start(bf16[4096,256]{1,0:T(8,128)(2,1)} %param.4) | copy-start | bytes 6291460
  9.3 29.0 %all-to-all-start = ((bf16[4,32,16,256]{3,2,1,0:T(8,128)(2,1)}), bf16[4,32,16,256]{3,2,1,0:T(8,128)(2,1)S(1)}, u32[]{:S(2)}, u32[]{:S(2)}) async-start(bf16[4,32,16,256]{3,2,1,0:T(8,128)(2,1)} %broadcast_in_dim.17), calls=%async_computation | async-start | bytes 2097152 | tf_op jit(solution)/shard_map/all_to_all | solution.py:44
  14.8 47.2 %all-gather.2.cloned.1.call-start = ((), (), s32[]{:S(2)}) async-start(), calls=%async_computation.5 | async-start | bytes 2359296 | tf_op jit(solution)/shard_map/all_gather | solution.py:88
  38.4 12.2 %collective-permute-start = (bf16[4,32,16,256]{3,2,1,0:T(8,128)(2,1)S(1)}, bf16[4,32,16,256]{3,2,1,0:T(8,128)(2,1)}, u32[]{:S(2)}, u32[]{:S(2)}) collective-permute-start(bf16[4,32,16,256]{3,2,1,0:T(8,128)(2,1)S(1)} %all-to-all-done), channel_id=1, source_target_pairs={{0,1},{1,0},{2,3},{3,2},{4,5},{5,4},{6,7},{7,6},{8,9},{9,8},{10,11... | collective-permute-start | bytes 3145736 | tf_op jit(solution)/shard_map/ppermute | solution.py:45
  135.6 2.3 copy-start.3
  135.6 3.0 %copy-start.4 = (bf16[4096,256]{1,0:T(8,128)(2,1)S(1)}, bf16[4096,256]{1,0:T(8,128)(2,1)}, u32[]{:S(2)}) copy-start(bf16[4096,256]{1,0:T(8,128)(2,1)} %param.5) | copy-start | bytes 6291460
  135.7 4.5 %copy-start.2 = (bf16[4,64,16,256]{3,2,1,0:T(8,128)(2,1)}, bf16[4,64,16,256]{3,2,1,0:T(8,128)(2,1)S(1)}, u32[]{:S(2)}) copy-start(bf16[4,64,16,256]{3,2,1,0:T(8,128)(2,1)S(1)} %copy.33) | copy-start | bytes 6291460
  140.3 1.4 copy-start.1
  143.2 64.9 %all-to-all-start.2 = ((bf16[4,64,16,256]{3,2,0,1:T(8,128)(2,1)}), bf16[4,64,16,256]{3,2,0,1:T(8,128)(2,1)}, u32[]{:S(2)}, u32[]{:S(2)}) async-start(bf16[4,64,16,256]{3,2,0,1:T(8,128)(2,1)} %copy.36), calls=%async_computation.2 | async-start | bytes 4194304 | tf_op jit(solution)/shard_map/all_to_all | solution.py:109
  150.7 106.1 %reduce-scatter.2.cloned.1.call-start = ((), (), s32[]{:S(2)}) async-start(), calls=%async_computation.6 | async-start | bytes 2359296 | tf_op jit(solution)/shard_map/reduce_scatter | solution.py:106
  212.6 12.1 %collective-permute-start.1 = (bf16[16,4,32,256]{3,2,0,1:T(8,128)(2,1)S(1)}, bf16[16,4,32,256]{3,2,0,1:T(8,128)(2,1)S(1)}, u32[]{:S(2)}, u32[]{:S(2)}) collective-permute-start(bf16[16,4,32,256]{3,2,0,1:T(8,128)(2,1)S(1)} %bitcast.64), channel_id=1, source_target_pairs={{0,1},{1,0},{2,3},{3,2},{4,5},{5,4},{6,7},{7,6},{8,9},{9,8},{10,11... | collective-permute-start | bytes 3145736 | tf_op jit(solution)/shard_map/ppermute | solution.py:61
Sparse Core Ops, SparseCore 0:
  17.7 44.2 all-gather.1
  159.9 61.8 reduce-scatter.1
